TPU v7x, 256 devices: a whole 4x4x8 slice. The times are simulated.
256 devices in a mesh: dp: 16 (over z, core), tensor: 16 (over y, x).
Axes of the slice: x: 4, y: 4, z: 8, core: 2. Of those that a mesh axis runs over, the one named last changes fastest.
Arguments:
- tokens: bfloat16 [8192, 2048], P(('dp', 'tensor')), may hold values from -6 to 6
- lengths: int32 [16, 8], P('dp'), may hold values from 1 to 128, 512 in all within a row
- group_prefix: int32 [16], replicated, may hold values from 0 to 15, as said below
- prefix_cache: bfloat16 [65536, 512], P(('dp', 'tensor')), may hold values from -340 to 340
- query_weight: bfloat16 [2048, 1024], P(None, 'tensor'), may hold values from -0.125 to 0.125
- key_weight: bfloat16 [2048, 256], replicated, may hold values from -0.375 to 0.375
- value_weight: bfloat16 [2048, 256], replicated, may hold values from -0.125 to 0.125
- out_weight: bfloat16 [1024, 2048], P('tensor'), may hold values from -0.1875 to 0.1875
- gate_up_weight: bfloat16 [2, 2048, 5120], P(None, None, 'tensor'), may hold values from -0.125 to 0.125
- down_weight: bfloat16 [5120, 2048], P('tensor'), may hold values from -0.078125 to 0.078125
Outputs:
- layer_out: bfloat16 [8192, 2048], P(('dp', 'tensor'))
Inputs may be any that keep to these rules, and one draw needn't show every extreme that they name: The 8 lengths of a group sum to 512, and one of them is exactly 128. `group_prefix`: several groups may continue the same slot.
All inputs are finite; a program needn't handle non-finite values.
Results may differ from a plain program's by a relative error of at most 0.023.
Values may be sent and summed in bfloat16 or wider, within the bound.
No kernel may reach another device: no remote copies, remote signals or barrier semaphores. Data moves between devices by JAX's collectives and lax.ppermute only.
A program may use at most 64 MiB of HBM per device.

v0:
```python
import math
import jax
import jax.numpy as jnp
from jax import lax
from jax.sharding import PartitionSpec as P

QH = 16
KVH = 4
HD = 64
PLEN = 4096
NEG_FILL = -1e30


def token_layout(lengths, total_rows):
    ends_at = jnp.cumsum(lengths)
    starts_at = ends_at - lengths
    indices = jnp.arange(total_rows, dtype=jnp.int32)
    request = jnp.sum((indices[:, None] >= ends_at[None, :]).astype(jnp.int32), axis=1)
    begins = jnp.max(
        jnp.where(starts_at[None, :] <= indices[:, None], starts_at[None, :], 0), axis=1
    )
    return ((PLEN + indices - begins).astype(jnp.float32), request)


def rope_tables(positions):
    halves = HD // 2
    steps_float = jnp.arange(halves, dtype=jnp.float32)
    inverse = jnp.exp(steps_float * (-2.0 * math.log(10000.0) / HD))
    angles = positions[:, None] * inverse[None, :]
    return (jnp.cos(angles), jnp.sin(angles))


def rotate(values, cos_table, sin_table):
    halves = values.shape[-1] // 2
    former = values[..., :halves]
    latter = values[..., halves:]
    cos_rows = cos_table[:, None, :]
    sin_rows = sin_table[:, None, :]
    return jnp.concatenate(
        [former * cos_rows - latter * sin_rows, latter * cos_rows + former * sin_rows], axis=-1
    )


def norm_rows(inputs):
    floats = inputs.astype(jnp.float32)
    return (floats * lax.rsqrt(jnp.mean(floats * floats, axis=-1, keepdims=True) + 1e-05)).astype(
        jnp.bfloat16
    )


def softmax_block(queries, keys_block, values_block, scaling, allowed):
    scores = (
        jnp.einsum("thd,nhd->thn", queries, keys_block, preferred_element_type=jnp.float32)
        * scaling
    )
    if allowed is not None:
        scores = jnp.where(allowed, scores, NEG_FILL)
    top_score = jnp.max(scores, axis=2)
    exponent = jnp.exp(scores - top_score[:, :, None])
    weight = jnp.sum(exponent, axis=2)
    blended = jnp.einsum(
        "thn,nhd->thd",
        exponent.astype(jnp.bfloat16),
        values_block,
        preferred_element_type=jnp.float32,
    )
    return (top_score, weight, blended)


def merge_states(former, latter):
    top_one, weight_one, blend_one = former
    top_two, weight_two, blend_two = latter
    overall = jnp.maximum(top_one, top_two)
    factor_one = jnp.exp(top_one - overall)
    factor_two = jnp.exp(top_two - overall)
    return (
        overall,
        weight_one * factor_one + weight_two * factor_two,
        blend_one * factor_one[:, :, None] + blend_two * factor_two[:, :, None],
    )


def on_device(
    tokens,
    lengths,
    group_prefix,
    prefix_cache,
    query_weight,
    key_weight,
    value_weight,
    out_weight,
    gate_up_weight,
    down_weight,
):
    tensor_count = lax.axis_size("tensor")
    tensor_rank = lax.axis_index("tensor")
    group_rank = lax.axis_index("dp")
    row_count = tokens.shape[0]
    group_tokens = row_count * tensor_count
    local_heads = query_weight.shape[1] // HD
    head_ratio = QH // KVH
    local_kv = max(1, local_heads // head_ratio)
    repeat_by = local_heads // local_kv
    kv_first = tensor_rank * local_heads // head_ratio
    kv_total = KVH * HD
    query_width = local_heads * HD
    kv_width = local_kv * HD
    scaling = 1.0 / math.sqrt(HD)
    positions, request = token_layout(lengths[0], group_tokens)
    cos_table, sin_table = rope_tables(positions)
    key_cols = lax.dynamic_slice_in_dim(key_weight, kv_first * HD, kv_width, 1)
    value_cols = lax.dynamic_slice_in_dim(value_weight, kv_first * HD, kv_width, 1)
    projection = jnp.concatenate([query_weight, key_cols, value_cols], axis=1)
    normed = norm_rows(tokens)
    segment = lax.all_gather(normed, "tensor", axis=0, tiled=True)
    seg_rows = segment.shape[0]
    mapped = jnp.dot(segment, projection, preferred_element_type=jnp.float32)
    query_part = rotate(
        mapped[:, :query_width].reshape(seg_rows, local_heads, HD), cos_table, sin_table
    )
    key_part = rotate(
        mapped[:, query_width : query_width + kv_width].reshape(seg_rows, local_kv, HD),
        cos_table,
        sin_table,
    )
    projected = jnp.concatenate(
        [
            query_part.reshape(seg_rows, query_width),
            key_part.reshape(seg_rows, kv_width),
            mapped[:, query_width + kv_width :],
        ],
        axis=1,
    ).astype(jnp.bfloat16)
    queries = projected[:, :query_width].reshape(group_tokens, local_heads, HD)
    own_keys = jnp.repeat(
        projected[:, query_width : query_width + kv_width].reshape(group_tokens, local_kv, HD),
        repeat_by,
        axis=1,
    )
    own_values = jnp.repeat(
        projected[:, query_width + kv_width :].reshape(group_tokens, local_kv, HD),
        repeat_by,
        axis=1,
    )
    slot_wanted = group_prefix[group_rank]
    shard_rows = prefix_cache.shape[0]
    segment = lax.all_gather(prefix_cache, "dp", axis=0, tiled=True)
    seg_rows = segment.shape[0]
    indices = jnp.arange(seg_rows, dtype=jnp.int32)
    matches = indices // shard_rows == slot_wanted
    places = indices % shard_rows
    chosen = (
        jnp.zeros_like(prefix_cache)
        .at[places]
        .add(jnp.where(matches[:, None], segment, jnp.zeros_like(segment)))
    )
    start_state = (
        jnp.full((group_tokens, local_heads), NEG_FILL, jnp.float32),
        jnp.zeros((group_tokens, local_heads), jnp.float32),
        jnp.zeros((group_tokens, local_heads, HD), jnp.float32),
    )
    segment = lax.all_gather(chosen, "tensor", axis=0, tiled=True)
    seg_rows = segment.shape[0]
    keys_block = lax.dynamic_slice_in_dim(segment, kv_first * HD, kv_width, 1).reshape(
        seg_rows, local_kv, HD
    )
    values_block = lax.dynamic_slice_in_dim(segment, kv_total + kv_first * HD, kv_width, 1).reshape(
        seg_rows, local_kv, HD
    )
    keys_block = jnp.repeat(keys_block, repeat_by, axis=1)
    values_block = jnp.repeat(values_block, repeat_by, axis=1)
    prefix_state = merge_states(
        start_state, softmax_block(queries, keys_block, values_block, scaling, None)
    )
    indices = jnp.arange(group_tokens, dtype=jnp.int32)
    allowed = (request[:, None] == request[None, :]) & (indices[None, :] <= indices[:, None])
    suffix_state = softmax_block(queries, own_keys, own_values, scaling, allowed[:, None, :])
    top_score, weight, blended = merge_states(prefix_state, suffix_state)
    attended = (
        (blended / weight[:, :, None]).astype(jnp.bfloat16).reshape(group_tokens, query_width)
    )
    attn_sum = lax.psum_scatter(
        jnp.dot(attended, out_weight, preferred_element_type=jnp.float32).astype(jnp.bfloat16),
        "tensor",
        scatter_dimension=0,
        tiled=True,
    ).astype(jnp.float32)
    middle = (tokens.astype(jnp.float32) + attn_sum).astype(jnp.bfloat16)
    segment = lax.all_gather(norm_rows(middle), "tensor", axis=0, tiled=True)
    gate_value = jnp.dot(segment, gate_up_weight[0], preferred_element_type=jnp.float32)
    upward = jnp.dot(segment, gate_up_weight[1], preferred_element_type=jnp.float32)
    hidden = (jax.nn.silu(gate_value) * upward).astype(jnp.bfloat16)
    ffn_sum = lax.psum_scatter(
        jnp.dot(hidden, down_weight, preferred_element_type=jnp.float32).astype(jnp.bfloat16),
        "tensor",
        scatter_dimension=0,
        tiled=True,
    ).astype(jnp.float32)
    return (middle.astype(jnp.float32) + ffn_sum).astype(jnp.bfloat16)


def solution(mesh):
    return jax.shard_map(
        on_device,
        mesh=mesh,
        in_specs=(
            P(("dp", "tensor"), None),
            P("dp", None),
            P(),
            P(("dp", "tensor"), None),
            P(None, "tensor"),
            P(),
            P(),
            P("tensor", None),
            P(None, None, "tensor"),
            P("tensor", None),
        ),
        out_specs=P(("dp", "tensor"), None),
        check_vma=False,
    )
```

profile of v0, /device:TPU:32, one launch (start us, length us, event | category | flops | bytes accessed | tf_op | source)
XLA Modules:
  0.0 400.2 jit_solution(4943395580398315689)
XLA Ops:
  6.5 0.0 copy-start
  6.5 0.0 all-gather.5.cloned.1.call-start
  6.5 0.7 all-gather.5.cloned.1.call-update
  7.3 0.0 all-gather.9.cloned.1.call-start
  7.3 1.0 fusion.66
  8.4 0.0 copy-start.3
  8.4 1.7 fusion.67
  10.1 0.0 all-gather.9.cloned.1.call-update
  10.1 0.0 all-gather.7.cloned.1.call-start
  10.1 1.2 dynamic_slice.15
  11.4 0.6 fusion.93
  12.0 41.6 %all-gather.5.cloned.1.call-done = bf16[4096,512]{1,0:T(8,128)(2,1)} async-done(((bf16[256,512]{1,0:T(8,128)(2,1)}), bf16[4096,512]{1,0:T(8,128)(2,1)}) %all-gather.5.cloned.1.call-update) | async-done | bytes 4194320 | tf_op jit(solution)/shard_map/all_gather | solution.py:147
  53.6 28.1 %scatter_custom_fusion = bf16[256,512]{1,0:T(8,128)(2,1)} fusion(s32[4096]{0:T(1024)S(1)} %bitcast.114, bf16[4096,512]{1,0:T(8,128)(2,1)} %all-gather.5.cloned.1.call-done, pred[4096]{0:T(1024)(128)(4,1)S(1)} %fusion.93, bf16[]{:T(256)} %constant.71.clone.1), kind=kCustom, calls=%fused_computation.7 | custom fusion | flops 4194304 | bytes 4461568 | tf_op jit(solution)/shard_map/scatter-add | solution.py:155
  81.8 0.0 all-gather.7.cloned.1.call-update
  81.8 0.0 reduce-scatter.3.cloned.1.call-start
  81.9 0.0 copy-done.5
  81.9 0.2 reduce-window.4
  82.1 0.3 copy.13
  82.4 0.1 select_reduce_fusion
  82.5 0.1 convert_reduce_fusion
  82.5 1.6 constant_dynamic-slice_fusion
  84.1 20.8 %all-gather.9.cloned.1.call-done = bf16[512,2048]{1,0:T(8,128)(2,1)} async-done(((bf16[32,2048]{1,0:T(8,128)(2,1)}), bf16[512,2048]{1,0:T(8,128)(2,1)}) %all-gather.9.cloned.1.call-update) | async-done | bytes 2097168 | tf_op jit(solution)/shard_map/all_gather | solution.py:115
  104.9 2.7 fusion.41
  107.7 0.3 fusion.86
  108.0 0.4 fusion.112
  108.4 0.2 fusion.51
  108.6 54.8 %all-gather.7.cloned.1.call-done = bf16[4096,512]{1,0:T(8,128)(2,1)} async-done(((bf16[256,512]{1,0:T(8,128)(2,1)}), bf16[4096,512]{1,0:T(8,128)(2,1)}) %all-gather.7.cloned.1.call-update) | async-done | bytes 4194320 | tf_op jit(solution)/shard_map/all_gather | solution.py:162
  163.4 2.5 multiply_reduce_fusion
  165.9 1.4 fusion.1
  167.4 0.0 copy-start.4
  167.4 3.1 fusion.36
  170.5 0.0 copy-done.4
  170.5 0.0 copy-start.1
  170.5 2.3 convolution_convert_fusion.1
  172.8 0.0 reduce-scatter.3.cloned.1.call-update
  172.9 0.0 all-gather.11.cloned.1.call-start
  172.9 79.3 %reduce-scatter.3.cloned.1.call-done = bf16[32,2048]{1,0:T(8,128)(2,1)} async-done(((bf16[512,2048]{1,0:T(8,128)(2,1)}), bf16[32,2048]{1,0:T(8,128)(2,1)}) %reduce-scatter.3.cloned.1.call-update) | async-done | bytes 131088 | tf_op jit(solution)/shard_map/reduce_scatter | solution.py:182
  252.2 0.0 copy-done.1
  252.2 1.1 fusion.69
  253.3 1.7 fusion.70
  255.0 0.0 all-gather.11.cloned.1.call-update
  255.0 0.2 reduce-scatter.5.cloned.1.call-start
  255.2 49.2 %all-gather.11.cloned.1.call-done = bf16[512,2048]{1,0:T(8,128)(2,1)} async-done(((bf16[32,2048]{1,0:T(8,128)(2,1)}), bf16[512,2048]{1,0:T(8,128)(2,1)}) %all-gather.11.cloned.1.call-update) | async-done | bytes 2097168 | tf_op jit(solution)/shard_map/all_gather | solution.py:189
  304.4 2.8 fusion.13
  307.2 5.5 %convolution_convert_fusion = bf16[512,2048]{1,0:T(8,128)(2,1)} fusion(bf16[320,2048]{1,0:T(8,128)(2,1)S(1)} %copy-done, bf16[512,2048]{1,0:T(8,128)(2,1)} %all-gather.11.cloned.1.call-done, bf16[2,2048,320]{1,2,0:T(8,128)(2,1)} %param.18, f32[512,320]{0,1:T(8,128)S(1)} %fusion.13), kind=kOutput, calls=%fused_computation.11 | convolution fusion | flops 1344208896 | bytes 7471104 | tf_op jit(solution)/shard_map/dot_general | solution.py:194
  312.7 0.0 reduce-scatter.5.cloned.1.call-update
  312.7 79.0 %reduce-scatter.5.cloned.1.call-done = bf16[32,2048]{1,0:T(8,128)(2,1)} async-done(((bf16[512,2048]{1,0:T(8,128)(2,1)}), bf16[32,2048]{1,0:T(8,128)(2,1)}) %reduce-scatter.5.cloned.1.call-update) | async-done | bytes 131088 | tf_op jit(solution)/shard_map/reduce_scatter | solution.py:193
  391.7 1.6 fusion.71
  (13 shorter events, 0.1 us)
Async XLA Ops:
  6.5 300.7 %copy-start = (bf16[320,2048]{1,0:T(8,128)(2,1)S(1)}, bf16[320,2048]{1,0:T(8,128)(2,1)}, u32[]{:S(2)}) copy-start(bf16[320,2048]{1,0:T(8,128)(2,1)} %param.19) | copy-start | bytes 3932164
  6.5 47.1 %all-gather.5.cloned.1.call-start = ((), (), s32[]{:S(2)}) async-start(), calls=%async_computation.2 | async-start | bytes 4456448 | tf_op jit(solution)/shard_map/all_gather | solution.py:147
  7.3 97.7 %all-gather.9.cloned.1.call-start = ((), (), s32[]{:S(2)}) async-start(), calls=%async_computation.4 | async-start | bytes 2228224 | tf_op jit(solution)/shard_map/all_gather | solution.py:115
  8.3 73.5 %copy-start.5 = (s32[1,8]{1,0:T(1,128)S(1)}, s32[1,8]{1,0:T(1,128)}, u32[]{:S(2)}) copy-start(s32[1,8]{1,0:T(1,128)} %param.11) | copy-start | bytes 100
  8.4 73.7 %copy-start.3 = (bf16[2048,64]{0,1:T(8,128)(2,1)S(1)}, bf16[2048,64]{0,1:T(8,128)(2,1)}, u32[]{:S(2)}) copy-start(bf16[2048,64]{0,1:T(8,128)(2,1)} %param.14) | copy-start | bytes 786436
  10.1 153.3 %all-gather.7.cloned.1.call-start = ((), (), s32[]{:S(2)}) async-start(), calls=%async_computation.3 | async-start | bytes 4456448 | tf_op jit(solution)/shard_map/all_gather | solution.py:162
  81.8 170.5 %reduce-scatter.3.cloned.1.call-start = ((), (), s32[]{:S(2)}) async-start(), calls=%async_computation.5 | async-start | bytes 2228224 | tf_op jit(solution)/shard_map/reduce_scatter | solution.py:182
  167.4 3.1 copy-start.4
  170.5 81.7 %copy-start.1 = (bf16[32,2048]{1,0:T(8,128)(2,1)S(1)}, bf16[32,2048]{1,0:T(8,128)(2,1)}, u32[]{:S(2)}) copy-start(bf16[32,2048]{1,0:T(8,128)(2,1)} %param.10) | copy-start | bytes 393220
  172.9 131.5 %all-gather.11.cloned.1.call-start = ((), (), s32[]{:S(2)}) async-start(), calls=%async_computation.6 | async-start | bytes 2228224 | tf_op jit(solution)/shard_map/all_gather | solution.py:189
  255.0 136.8 %reduce-scatter.5.cloned.1.call-start = ((), (), s32[]{:S(2)}) async-start(), calls=%async_computation.7 | async-start | bytes 2228224 | tf_op jit(solution)/shard_map/reduce_scatter | solution.py:193
  307.2 84.5 %copy-start.2 = (bf16[32,2048]{1,0:T(8,128)(2,1)S(1)}, bf16[32,2048]{1,0:T(8,128)(2,1)}, u32[]{:S(2)}) copy-start(bf16[32,2048]{1,0:T(8,128)(2,1)} %reduce-scatter.3.cloned.1.call-done) | copy-start | bytes 393220
Sparse Core Ops, SparseCore 0:
  9.2 44.4 all-gather.4
  56.1 48.8 all-gather.8
  107.4 55.9 all-gather.6
  173.0 79.2 reduce-scatter.2
  255.1 49.2 all-gather.10
  312.9 78.8 reduce-scatter.4
where the time goes:
time: 401 us; the launch traced here: 400 us
  waiting for transfers between devices  325 us (81%)
  other arithmetic  38.2 us (10%)
  matrix products  19.4 us (5%)
  between operations  13.7 us (3%)
    reduce_scatter x1, waiting for transfers between devices, on_device(): lax.psum_scatter(jnp.dot(attended, out_weight, preferred_element_type=jnp...  79.3 us
    reduce_scatter x1, waiting for transfers between devices, on_device(): lax.psum_scatter(jnp.dot(hidden, down_weight, preferred_element_type=jnp....  79 us
    all_gather x1, waiting for transfers between devices, on_device(): segment = lax.all_gather(chosen, 'tensor', axis=0, tiled=True)  54.8 us
    all_gather x1, waiting for transfers between devices, on_device(): segment = lax.all_gather(norm_rows(middle), 'tensor', axis=0, tiled=True)  49.2 us
    all_gather x1, waiting for transfers between devices, on_device(): segment = lax.all_gather(prefix_cache, 'dp', axis=0, tiled=True)  41.6 us
    scatter-add x1, other arithmetic, on_device(): chosen = jnp.zeros_like(prefix_cache).at[places].add(jnp.where(matches[:,...  28.1 us
    all_gather x1, waiting for transfers between devices, on_device(): segment = lax.all_gather(normed, 'tensor', axis=0, tiled=True)  20.8 us
  transfers between devices with their start and end apart: 6, of which 6 were waited for; matrix products, arithmetic and copies ran while one was open for 10% of the time, Pallas kernels for 0%

commit v1 on v0

--- a/solution.py
+++ b/solution.py
@@ -112,7 +112,10 @@
     value_cols = lax.dynamic_slice_in_dim(value_weight, kv_first * HD, kv_width, 1)
     projection = jnp.concatenate([query_weight, key_cols, value_cols], axis=1)
     normed = norm_rows(tokens)
-    segment = lax.all_gather(normed, "tensor", axis=0, tiled=True)
+    x_new = lax.axis_size("tensor")
+    new = jnp.stack(x_new * [normed], axis=0)
+    carry = lax.all_to_all(new, axis_name="tensor", split_axis=0, concat_axis=0)
+    segment = jnp.concatenate(carry, axis=0)
     seg_rows = segment.shape[0]
     mapped = jnp.dot(segment, projection, preferred_element_type=jnp.float32)
     query_part = rotate(

time: 401 us -> 389 us (0.970)
  waiting for transfers between devices: 325 us -> 308 us
  starting transfers between devices: 0.39 us -> 7.34 us
    all_to_all x0 -> x1, waiting for transfers between devices: none -> 34.6 us  [on_device(): carry = lax.all_to_all(new, axis_name='tensor', split_axis=0, concat_axis=0)]
    all_gather x1, waiting for transfers between devices: 54.8 us -> 20.7 us  [on_device(): segment = lax.all_gather(chosen, 'tensor', axis=0, tiled=True)]
    all_gather x1 -> x0, waiting for transfers between devices: 20.8 us -> none  [on_device(): segment = lax.all_gather(normed, 'tensor', axis=0, tiled=True)]
    all_to_all x0 -> x1, starting transfers between devices: none -> 6.99 us  [on_device(): carry = lax.all_to_all(new, axis_name='tensor', split_axis=0, concat_axis=0)]
  transfers between devices with their start and end apart: 6 -> 6, of which waited for: 6 -> 6; matrix products, arithmetic and copies ran while one was open for 10% -> 2% of each run, Pallas kernels for 0% -> 0%
where the time goes in v1:
time: 389 us; the launch traced here: 388 us
  waiting for transfers between devices  308 us (79%)
  other arithmetic  35.7 us (9%)
  matrix products  19.4 us (5%)
  between operations  13.3 us (3%)
  starting transfers between devices  7.34 us (2%)
  local copies, waits for them, and re-layouts  4.72 us (1%)
    reduce_scatter x1, waiting for transfers between devices, on_device(): lax.psum_scatter(jnp.dot(attended, out_weight, preferred_element_type=jnp...  79.2 us
    reduce_scatter x1, waiting for transfers between devices, on_device(): lax.psum_scatter(jnp.dot(hidden, down_weight, preferred_element_type=jnp....  78.9 us
    all_gather x1, waiting for transfers between devices, on_device(): segment = lax.all_gather(norm_rows(middle), 'tensor', axis=0, tiled=True)  49.2 us
    all_gather x1, waiting for transfers between devices, on_device(): segment = lax.all_gather(prefix_cache, 'dp', axis=0, tiled=True)  44.4 us
    all_to_all x1, waiting for transfers between devices, on_device(): carry = lax.all_to_all(new, axis_name='tensor', split_axis=0, concat_axis=0)  34.6 us
    scatter-add x1, other arithmetic, on_device(): chosen = jnp.zeros_like(prefix_cache).at[places].add(jnp.where(matches[:,...  28.1 us
    all_gather x1, waiting for transfers between devices, on_device(): segment = lax.all_gather(chosen, 'tensor', axis=0, tiled=True)  20.7 us
  transfers between devices with their start and end apart: 6, of which 6 were waited for; matrix products, arithmetic and copies ran while one was open for 2% of the time, Pallas kernels for 0%

profile of v1, /device:TPU:32, one launch (start us, length us, event | category | flops | bytes accessed | tf_op | source)
XLA Modules:
  0.0 388.3 jit_solution(10369378314448828358)
XLA Ops:
  6.5 0.0 copy-start
  6.5 0.0 all-gather.4.cloned.1.call-start
  6.5 0.7 all-gather.4.cloned.1.call-update
  7.3 0.0 all-gather.6.cloned.1.call-start
  7.3 1.2 dynamic_slice.15
  8.6 0.7 fusion.93
  9.2 44.4 %all-gather.4.cloned.1.call-done = bf16[4096,512]{1,0:T(8,128)(2,1)} async-done(((bf16[256,512]{1,0:T(8,128)(2,1)}), bf16[4096,512]{1,0:T(8,128)(2,1)}) %all-gather.4.cloned.1.call-update) | async-done | bytes 4194320 | tf_op jit(solution)/shard_map/all_gather | solution.py:150
  53.6 28.1 %scatter_custom_fusion = bf16[256,512]{1,0:T(8,128)(2,1)} fusion(s32[4096]{0:T(1024)S(1)} %bitcast.115, bf16[4096,512]{1,0:T(8,128)(2,1)} %all-gather.4.cloned.1.call-done, pred[4096]{0:T(1024)(128)(4,1)S(1)} %fusion.93, bf16[]{:T(256)} %constant.71.clone.1), kind=kCustom, calls=%fused_computation.7 | custom fusion | flops 4194304 | bytes 4461568 | tf_op jit(solution)/shard_map/scatter-add | solution.py:158
  81.8 0.0 all-gather.6.cloned.1.call-update
  81.8 0.0 copy-done.1
  81.8 0.1 fusion.66
  81.9 0.1 fusion.67
  82.1 1.6 stack.2
  83.7 7.0 %all-to-all-start = ((bf16[16,32,2048]{2,1,0:T(8,128)(2,1)}), bf16[16,32,2048]{2,1,0:T(8,128)(2,1)}, u32[]{:S(2)}, u32[]{:S(2)}) async-start(bf16[16,32,2048]{2,1,0:T(8,128)(2,1)} %stack.2), calls=%async_computation | async-start | bytes 4194304 | tf_op jit(solution)/shard_map/all_to_all | solution.py:117
  90.7 0.0 reduce-scatter.3.cloned.1.call-start
  90.7 0.0 copy-done.5
  90.7 0.2 reduce-window.4
  90.9 0.0 copy-done.3
  90.9 0.3 copy.13
  91.2 0.1 select_reduce_fusion
  91.3 0.1 convert_reduce_fusion
  91.4 1.6 constant_dynamic-slice_fusion
  93.0 34.6 %all-to-all-done = bf16[16,32,2048]{2,1,0:T(8,128)(2,1)} async-done(((bf16[16,32,2048]{2,1,0:T(8,128)(2,1)}), bf16[16,32,2048]{2,1,0:T(8,128)(2,1)}, u32[]{:S(2)}, u32[]{:S(2)}) %all-to-all-start) | async-done | bytes 2097184 | tf_op jit(solution)/shard_map/all_to_all | solution.py:117
  127.6 2.7 fusion.41
  130.3 0.3 fusion.86
  130.7 0.4 fusion.112
  131.1 0.2 fusion.51
  131.3 20.7 %all-gather.6.cloned.1.call-done = bf16[4096,512]{1,0:T(8,128)(2,1)} async-done(((bf16[256,512]{1,0:T(8,128)(2,1)}), bf16[4096,512]{1,0:T(8,128)(2,1)}) %all-gather.6.cloned.1.call-update) | async-done | bytes 4194320 | tf_op jit(solution)/shard_map/all_gather | solution.py:165
  152.0 2.5 multiply_reduce_fusion
  154.5 1.4 fusion.1
  156.0 0.0 copy-start.4
  156.0 3.1 fusion.36
  159.1 0.0 copy-done.4
  159.1 2.3 convolution_convert_fusion.1
  161.4 0.0 reduce-scatter.3.cloned.1.call-update
  161.4 0.0 all-gather.8.cloned.1.call-start
  161.5 79.2 %reduce-scatter.3.cloned.1.call-done = bf16[32,2048]{1,0:T(8,128)(2,1)} async-done(((bf16[512,2048]{1,0:T(8,128)(2,1)}), bf16[32,2048]{1,0:T(8,128)(2,1)}) %reduce-scatter.3.cloned.1.call-update) | async-done | bytes 131088 | tf_op jit(solution)/shard_map/reduce_scatter | solution.py:185
  240.7 1.1 fusion.69
  241.8 1.7 fusion.70
  243.5 0.0 all-gather.8.cloned.1.call-update
  243.5 0.2 reduce-scatter.5.cloned.1.call-start
  243.7 49.2 %all-gather.8.cloned.1.call-done = bf16[512,2048]{1,0:T(8,128)(2,1)} async-done(((bf16[32,2048]{1,0:T(8,128)(2,1)}), bf16[512,2048]{1,0:T(8,128)(2,1)}) %all-gather.8.cloned.1.call-update) | async-done | bytes 2097168 | tf_op jit(solution)/shard_map/all_gather | solution.py:192
  292.9 2.8 fusion.13
  295.7 5.5 %convolution_convert_fusion = bf16[512,2048]{1,0:T(8,128)(2,1)} fusion(bf16[320,2048]{1,0:T(8,128)(2,1)S(1)} %copy-done, bf16[512,2048]{1,0:T(8,128)(2,1)} %all-gather.8.cloned.1.call-done, bf16[2,2048,320]{1,2,0:T(8,128)(2,1)} %param.18, f32[512,320]{0,1:T(8,128)S(1)} %fusion.13), kind=kOutput, calls=%fused_computation.11 | convolution fusion | flops 1344208896 | bytes 7471104 | tf_op jit(solution)/shard_map/dot_general | solution.py:197
  301.2 0.0 reduce-scatter.5.cloned.1.call-update
  301.2 78.9 %reduce-scatter.5.cloned.1.call-done = bf16[32,2048]{1,0:T(8,128)(2,1)} async-done(((bf16[512,2048]{1,0:T(8,128)(2,1)}), bf16[32,2048]{1,0:T(8,128)(2,1)}) %reduce-scatter.5.cloned.1.call-update) | async-done | bytes 131088 | tf_op jit(solution)/shard_map/reduce_scatter | solution.py:196
  380.2 0.0 copy-done.2
  380.2 1.6 fusion.71
  (13 shorter events, 0.1 us)
Async XLA Ops:
  6.5 289.2 %copy-start = (bf16[320,2048]{1,0:T(8,128)(2,1)S(1)}, bf16[320,2048]{1,0:T(8,128)(2,1)}, u32[]{:S(2)}) copy-start(bf16[320,2048]{1,0:T(8,128)(2,1)} %param.19) | copy-start | bytes 3932164
  6.5 75.3 %copy-start.1 = (bf16[32,2048]{1,0:T(8,128)(2,1)S(1)}, bf16[32,2048]{1,0:T(8,128)(2,1)}, u32[]{:S(2)}) copy-start(bf16[32,2048]{1,0:T(8,128)(2,1)} %param.10) | copy-start | bytes 393220
  6.5 47.1 %all-gather.4.cloned.1.call-start = ((), (), s32[]{:S(2)}) async-start(), calls=%async_computation.3 | async-start | bytes 4456448 | tf_op jit(solution)/shard_map/all_gather | solution.py:150
  7.3 144.7 %all-gather.6.cloned.1.call-start = ((), (), s32[]{:S(2)}) async-start(), calls=%async_computation.4 | async-start | bytes 4456448 | tf_op jit(solution)/shard_map/all_gather | solution.py:165
  83.7 7.1 %copy-start.5 = (s32[1,8]{1,0:T(1,128)S(1)}, s32[1,8]{1,0:T(1,128)}, u32[]{:S(2)}) copy-start(s32[1,8]{1,0:T(1,128)} %param.11) | copy-start | bytes 100
  83.7 7.3 %copy-start.3 = (bf16[2048,64]{0,1:T(8,128)(2,1)S(1)}, bf16[2048,64]{0,1:T(8,128)(2,1)}, u32[]{:S(2)}) copy-start(bf16[2048,64]{0,1:T(8,128)(2,1)} %param.14) | copy-start | bytes 786436
  83.7 43.9 %all-to-all-start = ((bf16[16,32,2048]{2,1,0:T(8,128)(2,1)}), bf16[16,32,2048]{2,1,0:T(8,128)(2,1)}, u32[]{:S(2)}, u32[]{:S(2)}) async-start(bf16[16,32,2048]{2,1,0:T(8,128)(2,1)} %stack.2), calls=%async_computation | async-start | bytes 4194304 | tf_op jit(solution)/shard_map/all_to_all | solution.py:117
  90.7 150.1 %reduce-scatter.3.cloned.1.call-start = ((), (), s32[]{:S(2)}) async-start(), calls=%async_computation.5 | async-start | bytes 2228224 | tf_op jit(solution)/shard_map/reduce_scatter | solution.py:185
  156.0 3.1 copy-start.4
  161.4 131.4 %all-gather.8.cloned.1.call-start = ((), (), s32[]{:S(2)}) async-start(), calls=%async_computation.6 | async-start | bytes 2228224 | tf_op jit(solution)/shard_map/all_gather | solution.py:192
  243.5 136.7 %reduce-scatter.5.cloned.1.call-start = ((), (), s32[]{:S(2)}) async-start(), calls=%async_computation.7 | async-start | bytes 2228224 | tf_op jit(solution)/shard_map/reduce_scatter | solution.py:196
  295.7 84.4 %copy-start.2 = (bf16[32,2048]{1,0:T(8,128)(2,1)S(1)}, bf16[32,2048]{1,0:T(8,128)(2,1)}, u32[]{:S(2)}) copy-start(bf16[32,2048]{1,0:T(8,128)(2,1)} %reduce-scatter.3.cloned.1.call-done) | copy-start | bytes 393220
Sparse Core Ops, SparseCore 0:
  9.2 44.4 all-gather.3
  81.9 70.0 all-gather.5
  161.6 79.1 reduce-scatter.2
  243.6 49.2 all-gather.7
  301.4 78.7 reduce-scatter.4
